TPU v7x, 32 devices: a whole 2x2x4 slice. The times are simulated.
32 devices in a mesh: req: 8 (over z, y), ep: 4 (over x, core).
Axes of the slice: x: 2, y: 2, z: 4, core: 2. Of those that a mesh axis runs over, the one named last changes fastest.
Arguments:
- tokens: bfloat16 [4096, 1536], P(('req', 'ep')), may hold values from -6 to 6
- seg_ids: int32 [4096], P(('req', 'ep')), may hold values from 0 to 3, never falling along the last dimension, each value on 1 to 2048 neighbouring positions
- routes: int32 [4096, 8], P(('req', 'ep')), may hold values from 0 to 39, all different within a row; in each aligned block of 128 rows (0 to 127, 128 to 255, ...) at most 48 rows name the same one
- route_weights: float32 [4096, 8], P(('req', 'ep')), may hold values from 0.05 to 0.3
- norm1_gain: float32 [1536], replicated, may hold values from 0.5 to 1.5
- norm2_gain: float32 [1536], replicated, may hold values from 0.5 to 1.5
- w_query: bfloat16 [1536, 1536], P(None, 'ep')
- key_weight: bfloat16 [1536, 512], P(None, 'ep')
- value_weight: bfloat16 [1536, 512], P(None, 'ep'), may hold values from -0.15625 to 0.15625
- w_out_attn: bfloat16 [1536, 1536], P('ep'), may hold values from -0.15625 to 0.15625
- w_in: bfloat16 [40, 1536, 1024], P('ep'), may hold values from -0.15625 to 0.15625
- w_out: bfloat16 [40, 512, 1536], P('ep'), may hold values from -0.25 to 0.25
- paged_key_value_cache: bfloat16 [96, 8, 2, 64, 64], P('req', 'ep'), may hold values from -6 to 6
- page_table: int32 [64], replicated, may hold values from 0 to 95, as said below
Outputs:
- attn_out: bfloat16 [4096, 1536], P(('req', 'ep'))
- moe_out: bfloat16 [4096, 1536], P(('req', 'ep'))
- new_cache: bfloat16 [96, 8, 2, 64, 64], P('req', 'ep')
Inputs may be any that keep to these rules, and one draw needn't show every extreme that they name: `seg_ids`: segment ids never fall along the stream; the longest prompt holds exactly half of the 4096 tokens. `routes`: each token names 8 different experts; within the rows of one device no expert is named more than 48 times, a bound that some block reaches. `page_table`: entries are distinct.
All inputs are finite; a program needn't handle non-finite values.
Results may differ from a plain program's by a relative error of at most 0.017.
Values may be sent and summed in bfloat16 or wider, within the bound.
No kernel may reach another device: no remote copies, remote signals or barrier semaphores. Data moves between devices by JAX's collectives and lax.ppermute only.
A program may use at most 192 MiB of HBM per device.

v0:
```python
import jax
import jax.numpy as jnp
from jax import lax
from jax.sharding import PartitionSpec as P

HEAD_SIZE = 64
E = 40
PAGE_TOKENS = 64
CAP = 48


norm_eps = 1e-06
score_scale = 0.015625
residual_scale = 0.22
rope_base = 10000.0
neg_fill = -1e30


def rms_scale(rows, gain):
    mean_sq = jnp.mean(rows * rows, axis=-1, keepdims=True)
    return rows * lax.rsqrt(mean_sq + norm_eps) * gain


def positions_of(segments):
    tok_index = jnp.arange(segments.shape[0], dtype=jnp.int32)
    previous = jnp.concatenate([jnp.full((1,), -1, jnp.int32), segments[:-1]])
    starts = jnp.where(segments != previous, tok_index, 0)
    return tok_index - lax.cummax(starts, axis=0)


def rotary_apply(heads_in, token_positions):
    half_dim = heads_in.shape[-1] // 2
    inverse_freq = rope_base ** (
        -jnp.arange(half_dim, dtype=jnp.float32) * 2.0 / heads_in.shape[-1]
    )
    angles = token_positions.astype(jnp.float32)[:, None] * inverse_freq[None, :]
    cos_part = jnp.cos(angles)[:, None, :]
    sine_part = jnp.sin(angles)[:, None, :]
    first_half = heads_in[..., :half_dim]
    second_half = heads_in[..., half_dim:]
    return jnp.concatenate(
        [
            first_half * cos_part - second_half * sine_part,
            second_half * cos_part + first_half * sine_part,
        ],
        axis=-1,
    )


def body(
    tokens,
    seg_ids,
    routes,
    route_weights,
    norm1_gain,
    norm2_gain,
    w_query,
    key_weight,
    value_weight,
    w_out_attn,
    w_in,
    w_out,
    paged_key_value_cache,
    page_table,
):
    tok_dev = tokens.shape[0]
    ep_count = lax.axis_size("ep")
    group_len = tok_dev * ep_count
    req_pos = lax.axis_index("req")
    all_segs = lax.all_gather(seg_ids, ("req", "ep"), axis=0, tiled=True)
    all_pos = positions_of(all_segs)
    group_start = req_pos * group_len
    group_pos = lax.dynamic_slice_in_dim(all_pos, group_start, group_len)
    group_seg = lax.dynamic_slice_in_dim(all_segs, group_start, group_len)
    normed = rms_scale(tokens.astype(jnp.float32), norm1_gain).astype(jnp.bfloat16)
    joined = jnp.concatenate([w_query, key_weight, value_weight], axis=1)
    projected = jnp.dot(
        lax.all_gather(normed, "ep", axis=0, tiled=True), joined, preferred_element_type=jnp.float32
    )
    query_width = w_query.shape[1]
    kv_width = key_weight.shape[1]
    q_heads = query_width // HEAD_SIZE
    kv_heads = kv_width // HEAD_SIZE
    heads_ratio = q_heads // kv_heads
    query_rows = rotary_apply(
        projected[:, :query_width].reshape(group_len, q_heads, HEAD_SIZE), group_pos
    ).astype(jnp.bfloat16)
    key_matrix = (
        rotary_apply(
            projected[:, query_width : query_width + kv_width].reshape(
                group_len, kv_heads, HEAD_SIZE
            ),
            group_pos,
        )
        .astype(jnp.bfloat16)
        .reshape(group_len, kv_width)
    )
    value_rows = projected[:, query_width + kv_width :].astype(jnp.bfloat16)
    query_grouped = query_rows.reshape(group_len, kv_heads, heads_ratio, HEAD_SIZE).transpose(
        1, 2, 0, 3
    )
    pages_here = paged_key_value_cache.shape[0]
    page_first = req_pos * pages_here
    q_last = group_start + group_len - 1
    seg_low = group_seg[0]
    q_index = group_start + jnp.arange(group_len, dtype=jnp.int32)
    page_cells = kv_heads * 2 * PAGE_TOKENS * HEAD_SIZE
    cache_shape = paged_key_value_cache.shape
    local_pages = page_first + jnp.arange(pages_here, dtype=jnp.int32)
    begin_at = jnp.int32(0)
    run_max = jnp.full((kv_heads, heads_ratio, group_len), neg_fill, jnp.float32)
    run_sum = jnp.zeros((kv_heads, heads_ratio, group_len), jnp.float32)
    run_acc = jnp.zeros((kv_heads, heads_ratio, group_len, HEAD_SIZE), jnp.float32)
    cache_rows = paged_key_value_cache.reshape(pages_here, page_cells)
    key_piece = lax.all_gather(key_matrix, "req", axis=0, tiled=True)
    value_piece = lax.all_gather(value_rows, "req", axis=0, tiled=True)
    n_rows = key_piece.shape[0]
    piece_pages = n_rows // PAGE_TOKENS
    keys_paged = key_piece.reshape(piece_pages, PAGE_TOKENS, kv_heads, HEAD_SIZE).transpose(
        0, 2, 1, 3
    )
    values_paged = value_piece.reshape(piece_pages, PAGE_TOKENS, kv_heads, HEAD_SIZE).transpose(
        0, 2, 1, 3
    )
    fresh = jnp.stack([keys_paged, values_paged], axis=2).reshape(piece_pages, page_cells)
    match = local_pages[:, None] == page_table[None, :]
    placed = jnp.dot(match.astype(jnp.bfloat16), fresh, preferred_element_type=jnp.float32).astype(
        jnp.bfloat16
    )
    hit = jnp.any(match, axis=1)
    cache_rows = jnp.where(hit[:, None], placed, cache_rows)
    last_seg = lax.dynamic_index_in_dim(all_segs, begin_at + n_rows - 1, keepdims=False)
    needed = (begin_at <= q_last) & (last_seg >= seg_low)
    step_rows = min(n_rows, 1024)
    turns = n_rows // step_rows

    def attend(state_in):

        def one_block(turn_idx, state_now):
            block_max, block_sum, block_acc = state_now
            row_at = turn_idx * step_rows
            key_block = lax.dynamic_slice_in_dim(key_piece, row_at, step_rows).reshape(
                step_rows, kv_heads, HEAD_SIZE
            )
            value_block = lax.dynamic_slice_in_dim(value_piece, row_at, step_rows).reshape(
                step_rows, kv_heads, HEAD_SIZE
            )
            key_index = row_at + jnp.arange(step_rows, dtype=jnp.int32)
            key_segs = lax.dynamic_slice_in_dim(all_segs, row_at, step_rows)
            allowed = (group_seg[:, None] == key_segs[None, :]) & (
                key_index[None, :] <= q_index[:, None]
            )
            scores = (
                jnp.einsum(
                    "grqd,kgd->grqk", query_grouped, key_block, preferred_element_type=jnp.float32
                )
                * score_scale
            )
            masked = jnp.where(allowed, scores, neg_fill)
            new_max = jnp.maximum(block_max, jnp.max(masked, axis=-1))
            exponent = jnp.where(allowed, jnp.exp(masked - new_max[..., None]), 0.0)
            rescale = jnp.exp(block_max - new_max)
            new_sum = block_sum * rescale + jnp.sum(exponent, axis=-1)
            new_acc = block_acc * rescale[..., None] + jnp.einsum(
                "grqk,kgd->grqd",
                exponent.astype(jnp.bfloat16),
                value_block,
                preferred_element_type=jnp.float32,
            )
            return (new_max, new_sum, new_acc)

        return lax.fori_loop(0, turns, one_block, state_in)

    run_max, run_sum, run_acc = lax.cond(
        needed, attend, lambda state_in: state_in, (run_max, run_sum, run_acc)
    )
    run_max, run_sum, run_acc, cache_flat = (run_max, run_sum, run_acc, cache_rows)
    new_cache = cache_flat.reshape(cache_shape)
    head_out = (run_acc / run_sum[..., None]).astype(jnp.bfloat16)
    head_out = head_out.transpose(2, 0, 1, 3).reshape(group_len, query_width)
    attention = lax.psum_scatter(
        jnp.dot(head_out, w_out_attn, preferred_element_type=jnp.float32).astype(jnp.bfloat16),
        "ep",
        scatter_dimension=0,
        tiled=True,
    ).astype(jnp.float32)
    attn_out = attention.astype(jnp.bfloat16)
    moe_in = rms_scale(tokens.astype(jnp.float32) + residual_scale * attention, norm2_gain).astype(
        jnp.bfloat16
    )
    ffe_width = w_out.shape[1]
    exp_here = w_in.shape[0]
    expert_ids = jnp.arange(E, dtype=jnp.int32)
    shares = jnp.sum(
        jnp.where(routes[:, :, None] == expert_ids[None, None, :], route_weights[:, :, None], 0.0),
        axis=1,
    )
    rows_all = lax.all_gather(moe_in, "ep", axis=0, tiled=True)
    shares_all = lax.all_gather(shares, "ep", axis=0, tiled=True)
    first_expert = lax.axis_index("ep") * exp_here
    shares_here = lax.dynamic_slice_in_dim(shares_all, first_expert, exp_here, 1)
    total_rows = rows_all.shape[0]
    chosen = (shares_here > 0.0).astype(jnp.int32).reshape(ep_count, tok_dev, exp_here)
    slot_in = jnp.cumsum(chosen, axis=1) - 1
    source_ids = jnp.arange(ep_count, dtype=jnp.int32)[:, None, None]
    local_slot = (source_ids * CAP + slot_in).reshape(total_rows, exp_here)
    live = (chosen > 0).reshape(total_rows, exp_here)
    slot_ids = jnp.arange(ep_count * CAP, dtype=jnp.int32)
    dispatch = (local_slot.T[:, None, :] == slot_ids[None, :, None]) & live.T[:, None, :]
    arrived = jnp.einsum(
        "esr,rd->esd", dispatch.astype(jnp.bfloat16), rows_all, preferred_element_type=jnp.float32
    ).astype(jnp.bfloat16)
    gate_up = jnp.einsum("esd,edf->esf", arrived, w_in, preferred_element_type=jnp.float32)
    activated = (jax.nn.silu(gate_up[..., :ffe_width]) * gate_up[..., ffe_width:]).astype(
        jnp.bfloat16
    )
    result = jnp.einsum(
        "esf,efd->esd", activated, w_out, preferred_element_type=jnp.float32
    ).astype(jnp.bfloat16)
    slot_weight = jnp.sum(jnp.where(dispatch, shares_here.T[:, None, :], 0.0), axis=2)
    weighted = result.astype(jnp.float32) * slot_weight[..., None]
    partial_rows = jnp.einsum(
        "esr,esd->rd",
        dispatch.astype(jnp.float32),
        weighted,
        precision=lax.Precision.HIGHEST,
        preferred_element_type=jnp.float32,
    )
    moe_out = lax.psum_scatter(
        partial_rows.astype(jnp.bfloat16), "ep", scatter_dimension=0, tiled=True
    )
    return (attn_out, moe_out, new_cache)


def solution(mesh):
    in_specs = (
        P(("req", "ep"), None),
        P(("req", "ep")),
        P(("req", "ep"), None),
        P(("req", "ep"), None),
        P(),
        P(),
        P(None, "ep"),
        P(None, "ep"),
        P(None, "ep"),
        P("ep", None),
        P("ep", None, None),
        P("ep", None, None),
        P("req", "ep", None, None, None),
        P(),
    )
    out_specs = (P(("req", "ep"), None), P(("req", "ep"), None), P("req", "ep", None, None, None))
    return jax.shard_map(body, mesh=mesh, in_specs=in_specs, out_specs=out_specs, check_vma=False)
```

profile of v0, /device:TPU:12, one launch (start us, length us, event | category | flops | bytes accessed | tf_op | source)
XLA Modules:
  0.0 370.8 jit_solution(15703386580134532242)
XLA Ops:
  10.5 31.7 %all-gather = s32[32,1,128]{2,1,0:T(1,128)S(1)} all-gather(s32[1,1,128]{2,1,0:T(1,128)} %bitcast.115), channel_id=1, replica_groups=mesh['req'=8,'ep'=4] {'req','ep'}, dimensions={0}, use_global_device_ids=true | all-gather | bytes 16896 | tf_op jit(solution)/shard_map/all_gather | solution.py:70
  43.3 3.4 fusion.42
  52.8 40.3 %all-gather.8.cloned.1.call-done = bf16[4096,128]{0,1:T(8,128)(2,1)} async-done(((bf16[512,128]{0,1:T(8,128)(2,1)}), bf16[4096,128]{0,1:T(8,128)(2,1)}) %all-gather.8.cloned.1.call-update) | async-done | bytes 1048592 | tf_op jit(solution)/shard_map/all_gather | solution.py:115
  93.1 40.3 %all-gather.10.cloned.1.call-done = bf16[4096,128]{1,0:T(8,128)(2,1)} async-done(((bf16[512,128]{1,0:T(8,128)(2,1)}), bf16[4096,128]{1,0:T(8,128)(2,1)}) %all-gather.10.cloned.1.call-update) | async-done | bytes 1048592 | tf_op jit(solution)/shard_map/all_gather | solution.py:116
  133.4 99.9 %conditional.1 = (f32[2,3,512]{2,1,0:T(4,128)}, f32[2,3,512,64]{2,3,1,0:T(8,128)}) conditional(s32[]{:T(128)} %convert_element_type.66, () %tuple.30, (s32[]{:T(128)}, s32[512]{0:T(512)S(1)}, s32[512]{0:T(512)S(1)}, s32[4096]{0:T(1024)S(1)}, bf16[4096,128]{0,1:T(8,128)(2,1)}, /*index=5*/bf16[2,3,512,64]{2,3,1,0:T(8,128)(2,1)S(1)}, ...), branch_computations={%region_3.4_spmd, %region_4.9_spmd} | conditional | flops 848380416 | bytes 44134744 | solution.py:174
  133.4 99.9 %while.17 = (s32[]{:T(128)}, f32[2,3,512]{2,1,0:T(4,128)S(1)}, f32[2,3,512]{2,1,0:T(4,128)}, f32[2,3,512,64]{2,3,1,0:T(8,128)}, s32[512]{0:T(512)S(1)}, /*index=...) while((s32[]{:T(128)}, f32[2,3,512]{2,1,0:T(4,128)S(1)}, ...), condition=%wide.region_8.8_spmd.clone, body=%wide.region_5.7_spmd.clone.sunk | while | flops 848379904 | bytes 44130508 | solution.py:172
  135.3 6.7 %fusion.87 = (f32[2,3,512]{2,1,0:T(4,128)S(1)}, f32[2,1024,3,512]{3,1,2,0:T(8,128)}) fusion(pred[512,1024]{0,1:T(8,128)(4,1)S(1)} %compare_and_fusion.2, bf16[1024,2,64,1]{0,2,3,1:T(8,128)(2,1)S(1)} %bitcast.98, bf16[2,3,512,64]{2,3,1,0:T(8,128)(2,1)S(1)} %get-tuple-element.398), kind=kOutput, calls=%fused_computation.2.clone.1 | convolution fusion | flops 412087296 | bytes 13774848 | tf_op jit(solution)/shard_map/cond/branch_1_fun/while/body/eval_jaxpr/grqd,kgd->grqk/dot_general | solution.py:154
  142.0 6.5 %fusion.88 = f32[2,3,512]{2,1,0:T(4,128)S(1)} fusion(f32[2,1024,3,512]{3,1,2,0:T(8,128)} %get-tuple-element.359, f32[2,3,512]{2,1,0:T(4,128)S(1)} %select_maximum_fusion.2, pred[512,1024]{0,1:T(8,128)(4,1)S(1)} %compare_and_fusion.2), kind=kLoop, calls=%fused_computation.4.clone.1 | loop fusion | flops 15725568 | bytes 13131776 | tf_op jit(solution)/shard_map/cond/branch_1_fun/while/body/eval_jaxpr/reduce_sum | solution.py:163
  150.3 7.4 %fusion.90 = f32[2,3,512,64]{2,3,1,0:T(8,128)} fusion(bf16[1024,2,64,1]{0,2,3,1:T(8,128)(2,1)S(1)} %bitcast.101, f32[2,1024,3,512]{3,1,2,0:T(8,128)} %get-tuple-element.359, f32[2,3,512]{2,1,0:T(4,128)S(1)} %select_maximum_fusion.2, pred[512,1024]{0,1:T(8,128)(4,1)S(1)} %compare_and_fusion.2, f32[2,3,512,64]{2,3,1,0:T(8,128)} %get-tuple-element.379, ...), kind=kOutput, calls=%fused_computation.8.clone.1 | convolution fusion | flops 418971648 | bytes 14966785 | tf_op jit(solution)/shard_map/cond/branch_1_fun/while/body/eval_jaxpr/grqk,kgd->grqd/dot_general | solution.py:164
  159.5 6.7 %fusion.87 = (f32[2,3,512]{2,1,0:T(4,128)S(1)}, f32[2,1024,3,512]{3,1,2,0:T(8,128)}) fusion(pred[512,1024]{0,1:T(8,128)(4,1)S(1)} %compare_and_fusion.2, bf16[1024,2,64,1]{0,2,3,1:T(8,128)(2,1)S(1)} %bitcast.98, bf16[2,3,512,64]{2,3,1,0:T(8,128)(2,1)S(1)} %get-tuple-element.398), kind=kOutput, calls=%fused_computation.2.clone.1 | convolution fusion | flops 412087296 | bytes 13774848 | tf_op jit(solution)/shard_map/cond/branch_1_fun/while/body/eval_jaxpr/grqd,kgd->grqk/dot_general | solution.py:154
  166.2 6.5 %fusion.88 = f32[2,3,512]{2,1,0:T(4,128)S(1)} fusion(f32[2,1024,3,512]{3,1,2,0:T(8,128)} %get-tuple-element.359, f32[2,3,512]{2,1,0:T(4,128)S(1)} %select_maximum_fusion.2, pred[512,1024]{0,1:T(8,128)(4,1)S(1)} %compare_and_fusion.2), kind=kLoop, calls=%fused_computation.4.clone.1 | loop fusion | flops 15725568 | bytes 13131776 | tf_op jit(solution)/shard_map/cond/branch_1_fun/while/body/eval_jaxpr/reduce_sum | solution.py:163
  175.3 7.6 %fusion.90 = f32[2,3,512,64]{2,3,1,0:T(8,128)} fusion(bf16[1024,2,64,1]{0,2,3,1:T(8,128)(2,1)S(1)} %bitcast.101, f32[2,1024,3,512]{3,1,2,0:T(8,128)} %get-tuple-element.359, f32[2,3,512]{2,1,0:T(4,128)S(1)} %select_maximum_fusion.2, pred[512,1024]{0,1:T(8,128)(4,1)S(1)} %compare_and_fusion.2, f32[2,3,512,64]{2,3,1,0:T(8,128)} %get-tuple-element.379, ...), kind=kOutput, calls=%fused_computation.8.clone.1 | convolution fusion | flops 418971648 | bytes 14966785 | tf_op jit(solution)/shard_map/cond/branch_1_fun/while/body/eval_jaxpr/grqk,kgd->grqd/dot_general | solution.py:164
  184.7 6.7 %fusion.87 = (f32[2,3,512]{2,1,0:T(4,128)S(1)}, f32[2,1024,3,512]{3,1,2,0:T(8,128)}) fusion(pred[512,1024]{0,1:T(8,128)(4,1)S(1)} %compare_and_fusion.2, bf16[1024,2,64,1]{0,2,3,1:T(8,128)(2,1)S(1)} %bitcast.98, bf16[2,3,512,64]{2,3,1,0:T(8,128)(2,1)S(1)} %get-tuple-element.398), kind=kOutput, calls=%fused_computation.2.clone.1 | convolution fusion | flops 412087296 | bytes 13774848 | tf_op jit(solution)/shard_map/cond/branch_1_fun/while/body/eval_jaxpr/grqd,kgd->grqk/dot_general | solution.py:154
  191.4 6.5 %fusion.88 = f32[2,3,512]{2,1,0:T(4,128)S(1)} fusion(f32[2,1024,3,512]{3,1,2,0:T(8,128)} %get-tuple-element.359, f32[2,3,512]{2,1,0:T(4,128)S(1)} %select_maximum_fusion.2, pred[512,1024]{0,1:T(8,128)(4,1)S(1)} %compare_and_fusion.2), kind=kLoop, calls=%fused_computation.4.clone.1 | loop fusion | flops 15725568 | bytes 13131776 | tf_op jit(solution)/shard_map/cond/branch_1_fun/while/body/eval_jaxpr/reduce_sum | solution.py:163
  200.4 7.6 %fusion.90 = f32[2,3,512,64]{2,3,1,0:T(8,128)} fusion(bf16[1024,2,64,1]{0,2,3,1:T(8,128)(2,1)S(1)} %bitcast.101, f32[2,1024,3,512]{3,1,2,0:T(8,128)} %get-tuple-element.359, f32[2,3,512]{2,1,0:T(4,128)S(1)} %select_maximum_fusion.2, pred[512,1024]{0,1:T(8,128)(4,1)S(1)} %compare_and_fusion.2, f32[2,3,512,64]{2,3,1,0:T(8,128)} %get-tuple-element.379, ...), kind=kOutput, calls=%fused_computation.8.clone.1 | convolution fusion | flops 418971648 | bytes 14966785 | tf_op jit(solution)/shard_map/cond/branch_1_fun/while/body/eval_jaxpr/grqk,kgd->grqd/dot_general | solution.py:164
  209.9 6.7 %fusion.87 = (f32[2,3,512]{2,1,0:T(4,128)S(1)}, f32[2,1024,3,512]{3,1,2,0:T(8,128)}) fusion(pred[512,1024]{0,1:T(8,128)(4,1)S(1)} %compare_and_fusion.2, bf16[1024,2,64,1]{0,2,3,1:T(8,128)(2,1)S(1)} %bitcast.98, bf16[2,3,512,64]{2,3,1,0:T(8,128)(2,1)S(1)} %get-tuple-element.398), kind=kOutput, calls=%fused_computation.2.clone.1 | convolution fusion | flops 412087296 | bytes 13774848 | tf_op jit(solution)/shard_map/cond/branch_1_fun/while/body/eval_jaxpr/grqd,kgd->grqk/dot_general | solution.py:154
  216.6 6.5 %fusion.88 = f32[2,3,512]{2,1,0:T(4,128)S(1)} fusion(f32[2,1024,3,512]{3,1,2,0:T(8,128)} %get-tuple-element.359, f32[2,3,512]{2,1,0:T(4,128)S(1)} %select_maximum_fusion.2, pred[512,1024]{0,1:T(8,128)(4,1)S(1)} %compare_and_fusion.2), kind=kLoop, calls=%fused_computation.4.clone.1 | loop fusion | flops 15725568 | bytes 13131776 | tf_op jit(solution)/shard_map/cond/branch_1_fun/while/body/eval_jaxpr/reduce_sum | solution.py:163
  225.6 7.6 %fusion.90 = f32[2,3,512,64]{2,3,1,0:T(8,128)} fusion(bf16[1024,2,64,1]{0,2,3,1:T(8,128)(2,1)S(1)} %bitcast.101, f32[2,1024,3,512]{3,1,2,0:T(8,128)} %get-tuple-element.359, f32[2,3,512]{2,1,0:T(4,128)S(1)} %select_maximum_fusion.2, pred[512,1024]{0,1:T(8,128)(4,1)S(1)} %compare_and_fusion.2, f32[2,3,512,64]{2,3,1,0:T(8,128)} %get-tuple-element.379, ...), kind=kOutput, calls=%fused_computation.8.clone.1 | convolution fusion | flops 418971648 | bytes 14966785 | tf_op jit(solution)/shard_map/cond/branch_1_fun/while/body/eval_jaxpr/grqk,kgd->grqd/dot_general | solution.py:164
  234.6 2.2 convolution_convert_fusion.1
  236.8 28.9 %reduce-scatter.3.cloned.1.call-done = bf16[128,1536]{1,0:T(8,128)(2,1)} async-done(((bf16[512,1536]{1,0:T(8,128)(2,1)}), bf16[128,1536]{1,0:T(8,128)(2,1)}) %reduce-scatter.3.cloned.1.call-update) | async-done | bytes 393232 | tf_op jit(solution)/shard_map/reduce_scatter | solution.py:181
  269.1 5.5 %all_gather.22 = f32[512,40]{0,1:T(8,128)S(1)} all-gather(f32[128,40]{0,1:T(8,128)S(1)} %select_reduce_fusion.1), channel_id=1, replica_groups=mesh['req'=8,'ep'=4] {'ep'}, dimensions={0}, use_global_device_ids=true | all-gather | bytes 102400 | tf_op jit(solution)/shard_map/all_gather | solution.py:199
  276.2 12.5 %all-gather.12.cloned.1.call-done = bf16[512,1536]{1,0:T(8,128)(2,1)} async-done(((bf16[128,1536]{1,0:T(8,128)(2,1)}), bf16[512,1536]{1,0:T(8,128)(2,1)}) %all-gather.12.cloned.1.call-update) | async-done | bytes 1572880 | tf_op jit(solution)/shard_map/all_gather | solution.py:198
  288.8 17.3 %fusion.19 = f32[10,192,1024]{2,1,0:T(8,128)} fusion(bf16[10,1536,1024]{2,1,0:T(8,128)(2,1)} %param.28, s32[10,512]{1,0:T(8,128)S(1)} %copy.55, pred[10,512]{1,0:T(8,128)(4,1)S(1)} %get-tuple-element.283, bf16[512,1536]{1,0:T(8,128)(2,1)} %all-gather.12.cloned.1.call-done), kind=kOutput, calls=%fused_computation.28 | convolution fusion | flops 9064611840 | bytes 40920064 | tf_op jit(solution)/shard_map/esd,edf->esf/dot_general | solution.py:213
  306.0 13.6 %fusion.40 = bf16[10,192,1536]{2,1,0:T(8,128)(2,1)} fusion(bf16[10,512,1536]{2,1,0:T(8,128)(2,1)} %param.29, f32[10,192,1024]{2,1,0:T(8,128)} %fusion.19), kind=kOutput, calls=%fused_computation.41 | convolution fusion | flops 3025797120 | bytes 29491200 | tf_op jit(solution)/shard_map/esf,efd->esd/dot_general | solution.py:217
  319.7 15.9 %fusion.35 = bf16[512,1536]{1,0:T(8,128)(2,1)} fusion(f32[10,192]{1,0:T(8,128)S(1)} %select_reduce_fusion, bf16[10,192,1536]{2,1,0:T(8,128)(2,1)} %fusion.40, s32[10,512]{1,0:T(8,128)S(1)} %copy.55, pred[10,512]{1,0:T(8,128)(4,1)S(1)} %get-tuple-element.283), kind=kOutput, calls=%fused_computation.38 | convolution fusion | flops 18128044032 | bytes 7504384 | tf_op jit(solution)/shard_map/esr,esd->rd/dot_general | solution.py:222
  337.3 2.3 reshape.178
  339.6 3.0 copy.56
  345.1 2.7 pad_maximum_fusion
  347.9 5.0 %reshape.180 = bf16[64,16384]{1,0:T(8,128)(2,1)S(1)} reshape(bf16[64,2,2,64,64]{4,3,2,1,0:T(8,128)(2,1)} %pad_maximum_fusion) | data formatting | bytes 4194304 | tf_op jit(solution)/shard_map/reshape | solution.py:125
  352.8 2.3 fusion.13
  355.1 2.7 reshape.182
  357.8 6.1 %reduce-scatter.5.cloned.1.call-done = bf16[128,1536]{1,0:T(8,128)(2,1)} async-done(((bf16[512,1536]{1,0:T(8,128)(2,1)}), bf16[128,1536]{1,0:T(8,128)(2,1)}) %reduce-scatter.5.cloned.1.call-update) | async-done | bytes 393232 | tf_op jit(solution)/shard_map/reduce_scatter | solution.py:229
  (122 shorter events, 36.0 us)
Async XLA Ops:
  7.2 227.4 %copy-start = (bf16[384,1536]{1,0:T(8,128)(2,1)S(1)}, bf16[384,1536]{1,0:T(8,128)(2,1)}, u32[]{:S(2)}) copy-start(bf16[384,1536]{1,0:T(8,128)(2,1)} %param.27) | copy-start | bytes 3538948
  7.2 36.1 %all-gather.6.cloned.1.call-start = ((), (), s32[]{:S(2)}) async-start(), calls=%async_computation.2 | async-start | bytes 1966080 | tf_op jit(solution)/shard_map/all_gather | solution.py:78
  10.4 82.7 %all-gather.8.cloned.1.call-start = ((), (), s32[]{:S(2)}) async-start(), calls=%async_computation.3 | async-start | bytes 1179648 | tf_op jit(solution)/shard_map/all_gather | solution.py:115
  46.7 4.4 %copy-start.6 = (f32[512,640]{1,0:T(8,128)}, f32[512,640]{1,0:T(8,128)S(1)}, u32[]{:S(2)}) copy-start(f32[512,640]{1,0:T(8,128)S(1)} %fusion.42) | copy-start | bytes 3932164
  47.8 85.6 %all-gather.10.cloned.1.call-start = ((), (), s32[]{:S(2)}) async-start(), calls=%async_computation.4 | async-start | bytes 1179648 | tf_op jit(solution)/shard_map/all_gather | solution.py:116
  48.6 217.2 %reduce-scatter.3.cloned.1.call-start = ((), (), s32[]{:S(2)}) async-start(), calls=%async_computation.5 | async-start | bytes 1966080 | tf_op jit(solution)/shard_map/reduce_scatter | solution.py:181
  233.3 32.5 %copy-start.3 = (bf16[128,1536]{1,0:T(8,128)(2,1)S(1)}, bf16[128,1536]{1,0:T(8,128)(2,1)}, u32[]{:S(2)}) copy-start(bf16[128,1536]{1,0:T(8,128)(2,1)} %param.18) | copy-start | bytes 1179652
  233.3 33.7 %copy-start.8 = (f32[1536]{0:T(1024)S(1)}, f32[1536]{0:T(1024)}, u32[]{:S(2)}) copy-start(f32[1536]{0:T(1024)} %param.23) | copy-start | bytes 18436
  233.3 35.7 %copy-start.9 = (f32[128,8]{0,1:T(8,128)S(1)}, f32[128,8]{0,1:T(8,128)}, u32[]{:S(2)}) copy-start(f32[128,8]{0,1:T(8,128)} %param.21) | copy-start | bytes 12292
  233.3 35.7 %copy-start.10 = (s32[128,8]{0,1:T(8,128)S(1)}, s32[128,8]{0,1:T(8,128)}, u32[]{:S(2)}) copy-start(s32[128,8]{0,1:T(8,128)} %param.20) | copy-start | bytes 12292
  236.8 52.0 %all-gather.12.cloned.1.call-start = ((), (), s32[]{:S(2)}) async-start(), calls=%async_computation.6 | async-start | bytes 1966080 | tf_op jit(solution)/shard_map/all_gather | solution.py:198
  268.9 95.0 %reduce-scatter.5.cloned.1.call-start = ((), (), s32[]{:S(2)}) async-start(), calls=%async_computation.7 | async-start | bytes 1966080 | tf_op jit(solution)/shard_map/reduce_scatter | solution.py:229
  319.6 16.0 %copy-start.7 = (bf16[12,2,2,64,64]{4,3,2,1,0:T(8,128)(2,1)S(1)}, bf16[12,2,2,64,64]{4,3,2,1,0:T(8,128)(2,1)}, u32[]{:S(2)}) copy-start(bf16[12,2,2,64,64]{4,3,2,1,0:T(8,128)(2,1)} %param.30) | copy-start | bytes 1179652
  319.6 17.5 %copy-start.11 = (s32[64]{0:T(128)S(1)}, s32[64]{0:T(128)}, u32[]{:S(2)}) copy-start(s32[64]{0:T(128)} %param.31) | copy-start | bytes 772
  319.6 17.7 %copy-start.4 = (bf16[4096,128]{0,1:T(8,128)(2,1)S(1)}, bf16[4096,128]{0,1:T(8,128)(2,1)}, u32[]{:S(2)}) copy-start(bf16[4096,128]{0,1:T(8,128)(2,1)} %all-gather.8.cloned.1.call-done) | copy-start | bytes 3145732
  339.6 3.0 copy-start.5
  343.4 1.7 copy-start.2
  345.1 18.8 %copy-start.1 = (bf16[384,1536]{1,0:T(8,128)(2,1)S(1)}, bf16[384,1536]{1,0:T(8,128)(2,1)}, u32[]{:S(2)}) copy-start(bf16[384,1536]{1,0:T(8,128)(2,1)} %param.27) | copy-start | bytes 3538948
Sparse Core Ops, SparseCore 0:
  10.5 20.8 all-gather.5
  47.9 45.1 all-gather.7
  95.8 37.5 all-gather.9
  236.9 28.7 reduce-scatter.2
  269.1 19.6 all-gather.11
  335.7 28.1 reduce-scatter.4
where the time goes:
time: 373 us; the launch traced here: 371 us
  waiting for transfers between devices  128 us (34%)
  matrix products  112 us (30%)
  other arithmetic  48.2 us (13%)
  blocking collectives  37.2 us (10%)
  local copies, waits for them, and re-layouts  29.4 us (8%)
  between operations  15.7 us (4%)
    all_gather x1, waiting for transfers between devices, body(): key_piece = lax.all_gather(key_matrix, 'req', axis=0, tiled=True)  40.3 us
    all_gather x1, waiting for transfers between devices, body(): value_piece = lax.all_gather(value_rows, 'req', axis=0, tiled=True)  40.3 us
    all_gather x1, blocking collectives, body(): all_segs = lax.all_gather(seg_ids, ('req', 'ep'), axis=0, tiled=True)  31.7 us
    dot_general x4, matrix products, one_block(): jnp.einsum('grqk,kgd->grqd', exponent.astype(jnp.bfloat16), value_block,...  30.3 us
    reduce_scatter x1, waiting for transfers between devices, body(): lax.psum_scatter(jnp.dot(head_out, w_out_attn, preferred_element_type=jnp...  28.9 us
    dot_general x4, matrix products, one_block(): jnp.einsum('grqd,kgd->grqk', query_grouped, key_block, preferred_element_...  26.7 us
    reduce_sum x4, other arithmetic, one_block(): new_sum = block_sum * rescale + jnp.sum(exponent, axis=-1)  26.2 us
    dot_general x1, matrix products, body(): jnp.einsum('esd,edf->esf', arrived, w_in, preferred_element_type=jnp.floa...  17.3 us
  transfers between devices with their start and end apart: 6, of which 5 were waited for; matrix products, arithmetic and copies ran while one was open for 7% of the time, Pallas kernels for 0%

commit v1 on v0

--- a/solution.py
+++ b/solution.py
@@ -2,6 +2,8 @@
 import jax.numpy as jnp
 from jax import lax
 from jax.sharding import PartitionSpec as P
+from jax.experimental import pallas as pl
+from jax.experimental.pallas import tpu as pltpu
 
 HEAD_SIZE = 64
 E = 40
@@ -45,6 +47,79 @@
         ],
         axis=-1,
     )
+
+
+Q_TILE = 128
+K_TILE = 256
+
+
+def flash_body(lo_ref, hi_ref, q_ref, k_ref, v_ref, tok_ref, begin_ref, o_ref):
+    qb = pl.program_id(1)
+    ratio = q_ref.shape[1]
+    q_tile = q_ref.shape[2]
+    head_dim = q_ref.shape[3]
+    q = q_ref[0].reshape(ratio * q_tile, head_dim)
+    tok = tok_ref[...]
+    begin = begin_ref[...]
+
+    def step(kb, carry):
+        m_old, l_old, acc_old = carry
+        k0 = pl.multiple_of(kb * K_TILE, K_TILE)
+        k_blk = k_ref[0, pl.ds(k0, K_TILE), :]
+        v_blk = v_ref[0, pl.ds(k0, K_TILE), :]
+        s = lax.dot_general(
+            q, k_blk, (((1,), (1,)), ((), ())), preferred_element_type=jnp.float32
+        )
+        s = (s * score_scale).reshape(ratio, q_tile, K_TILE)
+        key_at = k0 + lax.broadcasted_iota(jnp.int32, (q_tile, K_TILE), 1)
+        allowed = (key_at >= begin) & (key_at <= tok)
+        s = jnp.where(allowed[None], s, -jnp.inf)
+        m_new = jnp.maximum(m_old, jnp.max(s, axis=-1, keepdims=True))
+        alpha = jnp.exp(m_old - m_new)
+        p = jnp.exp(s - m_new)
+        l_new = alpha * l_old + jnp.sum(p, axis=-1, keepdims=True)
+        pv = lax.dot_general(
+            p.reshape(ratio * q_tile, K_TILE).astype(jnp.bfloat16),
+            v_blk,
+            (((1,), (0,)), ((), ())),
+            preferred_element_type=jnp.float32,
+        )
+        acc_new = alpha * acc_old + pv.reshape(ratio, q_tile, head_dim)
+        return m_new, l_new, acc_new
+
+    init = (
+        jnp.full((ratio, q_tile, 1), neg_fill, jnp.float32),
+        jnp.zeros((ratio, q_tile, 1), jnp.float32),
+        jnp.zeros((ratio, q_tile, head_dim), jnp.float32),
+    )
+    m_fin, l_fin, acc_fin = lax.fori_loop(lo_ref[qb], hi_ref[qb] + 1, step, init)
+    o_ref[0] = (acc_fin / l_fin).astype(o_ref.dtype)
+
+
+def flash_attention(query_grouped, kv_all, q_index, q_begin):
+    kv_heads, ratio, group_len, head_dim = query_grouped.shape
+    n_rows = kv_all.shape[1]
+    n_q = group_len // Q_TILE
+    lo = jnp.min(q_begin.reshape(n_q, Q_TILE), axis=1) // K_TILE
+    hi = jnp.max(q_index.reshape(n_q, Q_TILE), axis=1) // K_TILE
+    grid_spec = pltpu.PrefetchScalarGridSpec(
+        num_scalar_prefetch=2,
+        grid=(kv_heads, n_q),
+        in_specs=[
+            pl.BlockSpec((1, ratio, Q_TILE, head_dim), lambda g, qb, lo, hi: (g, 0, qb, 0)),
+            pl.BlockSpec((1, n_rows, head_dim), lambda g, qb, lo, hi: (g, 0, 0)),
+            pl.BlockSpec((1, n_rows, head_dim), lambda g, qb, lo, hi: (kv_heads + g, 0, 0)),
+            pl.BlockSpec((Q_TILE, 1), lambda g, qb, lo, hi: (qb, 0)),
+            pl.BlockSpec((Q_TILE, 1), lambda g, qb, lo, hi: (qb, 0)),
+        ],
+        out_specs=pl.BlockSpec((1, ratio, Q_TILE, head_dim), lambda g, qb, lo, hi: (g, 0, qb, 0)),
+    )
+    out = pl.pallas_call(
+        flash_body,
+        grid_spec=grid_spec,
+        out_shape=jax.ShapeDtypeStruct(query_grouped.shape, jnp.bfloat16),
+    )(lo, hi, query_grouped, kv_all, kv_all, q_index[:, None], q_begin[:, None])
+    return out
 
 
 def body(
@@ -85,98 +160,38 @@
     query_rows = rotary_apply(
         projected[:, :query_width].reshape(group_len, q_heads, HEAD_SIZE), group_pos
     ).astype(jnp.bfloat16)
-    key_matrix = (
-        rotary_apply(
-            projected[:, query_width : query_width + kv_width].reshape(
-                group_len, kv_heads, HEAD_SIZE
-            ),
-            group_pos,
-        )
+    key_rows = rotary_apply(
+        projected[:, query_width : query_width + kv_width].reshape(
+            group_len, kv_heads, HEAD_SIZE
+        ),
+        group_pos,
+    ).astype(jnp.bfloat16)
+    value_rows = (
+        projected[:, query_width + kv_width :]
         .astype(jnp.bfloat16)
-        .reshape(group_len, kv_width)
-    )
-    value_rows = projected[:, query_width + kv_width :].astype(jnp.bfloat16)
+        .reshape(group_len, kv_heads, HEAD_SIZE)
+    )
     query_grouped = query_rows.reshape(group_len, kv_heads, heads_ratio, HEAD_SIZE).transpose(
         1, 2, 0, 3
     )
+    kv_local = jnp.concatenate(
+        [key_rows.transpose(1, 0, 2), value_rows.transpose(1, 0, 2)], axis=0
+    )
+    kv_all = lax.all_gather(kv_local, "req", axis=1, tiled=True)
+    n_rows = kv_all.shape[1]
+    q_index = group_start + jnp.arange(group_len, dtype=jnp.int32)
+    q_begin = q_index - group_pos
+    head_out = flash_attention(query_grouped, kv_all, q_index, q_begin)
     pages_here = paged_key_value_cache.shape[0]
     page_first = req_pos * pages_here
-    q_last = group_start + group_len - 1
-    seg_low = group_seg[0]
-    q_index = group_start + jnp.arange(group_len, dtype=jnp.int32)
-    page_cells = kv_heads * 2 * PAGE_TOKENS * HEAD_SIZE
-    cache_shape = paged_key_value_cache.shape
+    piece_pages = n_rows // PAGE_TOKENS
     local_pages = page_first + jnp.arange(pages_here, dtype=jnp.int32)
-    begin_at = jnp.int32(0)
-    run_max = jnp.full((kv_heads, heads_ratio, group_len), neg_fill, jnp.float32)
-    run_sum = jnp.zeros((kv_heads, heads_ratio, group_len), jnp.float32)
-    run_acc = jnp.zeros((kv_heads, heads_ratio, group_len, HEAD_SIZE), jnp.float32)
-    cache_rows = paged_key_value_cache.reshape(pages_here, page_cells)
-    key_piece = lax.all_gather(key_matrix, "req", axis=0, tiled=True)
-    value_piece = lax.all_gather(value_rows, "req", axis=0, tiled=True)
-    n_rows = key_piece.shape[0]
-    piece_pages = n_rows // PAGE_TOKENS
-    keys_paged = key_piece.reshape(piece_pages, PAGE_TOKENS, kv_heads, HEAD_SIZE).transpose(
-        0, 2, 1, 3
-    )
-    values_paged = value_piece.reshape(piece_pages, PAGE_TOKENS, kv_heads, HEAD_SIZE).transpose(
-        0, 2, 1, 3
-    )
-    fresh = jnp.stack([keys_paged, values_paged], axis=2).reshape(piece_pages, page_cells)
     match = local_pages[:, None] == page_table[None, :]
-    placed = jnp.dot(match.astype(jnp.bfloat16), fresh, preferred_element_type=jnp.float32).astype(
-        jnp.bfloat16
-    )
     hit = jnp.any(match, axis=1)
-    cache_rows = jnp.where(hit[:, None], placed, cache_rows)
-    last_seg = lax.dynamic_index_in_dim(all_segs, begin_at + n_rows - 1, keepdims=False)
-    needed = (begin_at <= q_last) & (last_seg >= seg_low)
-    step_rows = min(n_rows, 1024)
-    turns = n_rows // step_rows
-
-    def attend(state_in):
-
-        def one_block(turn_idx, state_now):
-            block_max, block_sum, block_acc = state_now
-            row_at = turn_idx * step_rows
-            key_block = lax.dynamic_slice_in_dim(key_piece, row_at, step_rows).reshape(
-                step_rows, kv_heads, HEAD_SIZE
-            )
-            value_block = lax.dynamic_slice_in_dim(value_piece, row_at, step_rows).reshape(
-                step_rows, kv_heads, HEAD_SIZE
-            )
-            key_index = row_at + jnp.arange(step_rows, dtype=jnp.int32)
-            key_segs = lax.dynamic_slice_in_dim(all_segs, row_at, step_rows)
-            allowed = (group_seg[:, None] == key_segs[None, :]) & (
-                key_index[None, :] <= q_index[:, None]
-            )
-            scores = (
-                jnp.einsum(
-                    "grqd,kgd->grqk", query_grouped, key_block, preferred_element_type=jnp.float32
-                )
-                * score_scale
-            )
-            masked = jnp.where(allowed, scores, neg_fill)
-            new_max = jnp.maximum(block_max, jnp.max(masked, axis=-1))
-            exponent = jnp.where(allowed, jnp.exp(masked - new_max[..., None]), 0.0)
-            rescale = jnp.exp(block_max - new_max)
-            new_sum = block_sum * rescale + jnp.sum(exponent, axis=-1)
-            new_acc = block_acc * rescale[..., None] + jnp.einsum(
-                "grqk,kgd->grqd",
-                exponent.astype(jnp.bfloat16),
-                value_block,
-                preferred_element_type=jnp.float32,
-            )
-            return (new_max, new_sum, new_acc)
-
-        return lax.fori_loop(0, turns, one_block, state_in)
-
-    run_max, run_sum, run_acc = lax.cond(
-        needed, attend, lambda state_in: state_in, (run_max, run_sum, run_acc)
-    )
-    run_max, run_sum, run_acc, cache_flat = (run_max, run_sum, run_acc, cache_rows)
-    new_cache = cache_flat.reshape(cache_shape)
-    head_out = (run_acc / run_sum[..., None]).astype(jnp.bfloat16)
+    block_of = jnp.argmax(match, axis=1).astype(jnp.int32)
+    kv_paged = kv_all.reshape(2, kv_heads, piece_pages, PAGE_TOKENS, HEAD_SIZE)
+    picked = jnp.take(kv_paged, block_of, axis=2, mode="clip").transpose(2, 1, 0, 3, 4)
+    new_cache = jnp.where(hit[:, None, None, None, None], picked, paged_key_value_cache)
     head_out = head_out.transpose(2, 0, 1, 3).reshape(group_len, query_width)
     attention = lax.psum_scatter(
         jnp.dot(head_out, w_out_attn, preferred_element_type=jnp.float32).astype(jnp.bfloat16),

time: 373 us -> 300 us (0.80)
  matrix products: 112 us -> 52.4 us
  other arithmetic: 48.2 us -> 13.9 us
  waiting for transfers between devices: 128 us -> 153 us
  local copies, waits for them, and re-layouts: 29.4 us -> 11 us
  Pallas kernels: 0 us -> 17.1 us
    dot_general x9 -> x0, matrix products: 59.3 us -> none  [the longest x4 30.3 us: one_block(): jnp.einsum('grqk,kgd->grqd', exponent.astype(jnp.bfloat16), value_block,...]
    reduce_sum x4 -> x0, other arithmetic: 26.2 us -> none  [one_block(): new_sum = block_sum * rescale + jnp.sum(exponent, axis=-1)]
    reduce_scatter x1, waiting for transfers between devices: 6.11 us -> 23.4 us  [body(): lax.psum_scatter(partial_rows.astype(jnp.bfloat16), 'ep', scatter_dimensi...]
    pallas_call x0 -> x1, Pallas kernels: none -> 17.1 us  [flash_attention(): pl.pallas_call(flash_body, grid_spec=grid_spec, out_shape=jax.ShapeDtypeS...]
    reduce_scatter x1, waiting for transfers between devices: 28.9 us -> 45 us  [body(): lax.psum_scatter(jnp.dot(head_out, w_out_attn, preferred_element_type=jnp...]
    reshape x7 -> x1, local copies, waits for them, and re-layouts: 15.8 us -> 0.17 us  [body(): value_rows = projected[:, query_width + kv_width:].astype(jnp.bfloat16).r...]
    dynamic_slice x18 -> x0, local copies, waits for them, and re-layouts: 9.02 us -> none  [the longest x8 4.44 us: one_block(): lax.dynamic_slice_in_dim(value_piece, row_at, step_rows)]
    all_gather x2 -> x1, waiting for transfers between devices: 80.6 us -> 71.7 us  [body(): kv_all = lax.all_gather(kv_local, 'req', axis=1, tiled=True)]
  transfers between devices with their start and end apart: 6 -> 5, of which waited for: 5 -> 4; matrix products, arithmetic and copies ran while one was open for 7% -> 5% of each run, Pallas kernels for 0% -> 0%
where the time goes in v1:
time: 300 us; the launch traced here: 299 us
  waiting for transfers between devices  153 us (51%)
  matrix products  52.4 us (17%)
  blocking collectives  37.2 us (12%)
  Pallas kernels  17.1 us (6%)
  between operations  14.1 us (5%)
  other arithmetic  13.9 us (5%)
  local copies, waits for them, and re-layouts  11 us (4%)
    all_gather x1, waiting for transfers between devices, body(): kv_all = lax.all_gather(kv_local, 'req', axis=1, tiled=True)  71.7 us
    reduce_scatter x1, waiting for transfers between devices, body(): lax.psum_scatter(jnp.dot(head_out, w_out_attn, preferred_element_type=jnp...  45 us
    all_gather x1, blocking collectives, body(): all_segs = lax.all_gather(seg_ids, ('req', 'ep'), axis=0, tiled=True)  31.7 us
    reduce_scatter x1, waiting for transfers between devices, body(): lax.psum_scatter(partial_rows.astype(jnp.bfloat16), 'ep', scatter_dimensi...  23.4 us
    dot_general x1, matrix products, body(): jnp.einsum('esd,edf->esf', arrived, w_in, preferred_element_type=jnp.floa...  17.3 us
    pallas_call x1, Pallas kernels, flash_attention(): pl.pallas_call(flash_body, grid_spec=grid_spec, out_shape=jax.ShapeDtypeS...  17.1 us
    dot_general x1, matrix products, body(): jnp.einsum('esr,esd->rd', dispatch.astype(jnp.float32), weighted, precisi...  15.9 us
    dot_general x1, matrix products, body(): jnp.einsum('esf,efd->esd', activated, w_out, preferred_element_type=jnp.f...  13.6 us
  transfers between devices with their start and end apart: 5, of which 4 were waited for; matrix products, arithmetic and copies ran while one was open for 5% of the time, Pallas kernels for 0%

profile of v1, /device:TPU:12, one launch (start us, length us, event | category | flops | bytes accessed | tf_op | source)
XLA Modules:
  0.0 298.7 jit_solution(34167378140314554)
XLA Ops:
  7.2 1.2 fusion.43
  8.5 1.9 fusion.45
  10.5 31.7 %all-gather = s32[32,1,128]{2,1,0:T(1,128)S(1)} all-gather(s32[1,1,128]{2,1,0:T(1,128)} %bitcast.62), channel_id=1, replica_groups=mesh['req'=8,'ep'=4] {'req','ep'}, dimensions={0}, use_global_device_ids=true | all-gather | bytes 16896 | tf_op jit(solution)/shard_map/all_gather | solution.py:145
  42.3 0.3 reduce-window.9
  43.0 0.3 multiply_cosine_fusion
  43.6 3.4 %fusion.28 = f32[512,640]{1,0:T(8,128)S(1)} fusion(bf16[512,1536]{1,0:T(8,128)(2,1)} %all-gather.5.cloned.1.call-done, bf16[1536,128]{1,0:T(8,128)(2,1)} %param.22, bf16[1536,128]{1,0:T(8,128)(2,1)} %param.21, bf16[1536,384]{1,0:T(8,128)(2,1)} %param.20), kind=kOutput, calls=%fused_computation.18 | convolution fusion | flops 1012531200 | bytes 4849664 | tf_op jit(solution)/shard_map/dot_general | solution.py:152
  47.0 1.0 copy-done.3
  49.2 0.9 pad_maximum_fusion
  50.4 0.9 copy.88.begin_ref
  51.4 0.7 iota_add_fusion.tok_ref
  52.1 0.6 and_select_fusion
  52.7 1.2 slice.55
  54.3 0.4 copy.79
  54.7 0.4 copy.80
  55.1 1.3 maximum_bitcast_fusion.q_ref
  56.4 71.7 %all-gather.7.cloned.1.call-done.k_ref.v_ref = bf16[4,4096,64]{2,1,0:T(8,128)(2,1)} async-done(((bf16[4,512,64]{2,1,0:T(8,128)(2,1)}), bf16[4,4096,64]{2,1,0:T(8,128)(2,1)}) %all-gather.7.cloned.1.call-update) | async-done | bytes 2097168 | tf_op jit(solution)/shard_map/all_gather | solution.py:180
  128.1 17.1 %shard_map.157 = bf16[2,3,512,64]{3,2,1,0:T(8,128)(2,1)} custom-call(s32[4]{0:T(128)} %get-tuple-element.30.lo_ref, s32[4]{0:T(128)} %get-tuple-element.29.hi_ref, bf16[2,3,512,64]{3,2,1,0:T(8,128)(2,1)} %maximum_bitcast_fusion.q_ref, bf16[4,4096,64]{2,1,0:T(8,128)(2,1)} %all-gather.7.cloned.1.call-done.k_ref.v_ref, ...), custom_call_target="tpu_custom_call" | custom-call | tf_op jit(solution)/shard_map/pallas_call | solution.py:117
  145.3 1.4 copy.89
  146.7 2.2 convolution_convert_fusion
  149.0 45.0 %reduce-scatter.3.cloned.1.call-done = bf16[128,1536]{1,0:T(8,128)(2,1)} async-done(((bf16[512,1536]{1,0:T(8,128)(2,1)}), bf16[128,1536]{1,0:T(8,128)(2,1)}) %reduce-scatter.3.cloned.1.call-update) | async-done | bytes 393232 | tf_op jit(solution)/shard_map/reduce_scatter | solution.py:196
  194.0 1.2 multiply_reduce_fusion
  195.2 1.9 multiply_convert_fusion
  197.3 5.5 %all_gather.18 = f32[512,40]{0,1:T(8,128)S(1)} all-gather(f32[128,40]{0,1:T(8,128)S(1)} %select_reduce_fusion.1), channel_id=1, replica_groups=mesh['req'=8,'ep'=4] {'ep'}, dimensions={0}, use_global_device_ids=true | all-gather | bytes 102400 | tf_op jit(solution)/shard_map/all_gather | solution.py:214
  203.6 0.9 select_reduce_fusion
  204.5 12.5 %all-gather.9.cloned.1.call-done = bf16[512,1536]{1,0:T(8,128)(2,1)} async-done(((bf16[128,1536]{1,0:T(8,128)(2,1)}), bf16[512,1536]{1,0:T(8,128)(2,1)}) %all-gather.9.cloned.1.call-update) | async-done | bytes 1572880 | tf_op jit(solution)/shard_map/all_gather | solution.py:213
  217.0 17.3 %fusion.5 = f32[10,192,1024]{2,1,0:T(8,128)} fusion(bf16[10,1536,1024]{2,1,0:T(8,128)(2,1)} %param.24, s32[10,512]{1,0:T(8,128)S(1)} %copy.91, pred[10,512]{1,0:T(8,128)(4,1)S(1)} %get-tuple-element.17, bf16[512,1536]{1,0:T(8,128)(2,1)} %all-gather.9.cloned.1.call-done), kind=kOutput, calls=%fused_computation.6 | convolution fusion | flops 9064611840 | bytes 40920064 | tf_op jit(solution)/shard_map/esd,edf->esf/dot_general | solution.py:228
  234.3 13.6 %fusion.26 = bf16[10,192,1536]{2,1,0:T(8,128)(2,1)} fusion(bf16[10,512,1536]{2,1,0:T(8,128)(2,1)} %param.25, f32[10,192,1024]{2,1,0:T(8,128)} %fusion.5), kind=kOutput, calls=%fused_computation.17 | convolution fusion | flops 3025797120 | bytes 29491200 | tf_op jit(solution)/shard_map/esf,efd->esd/dot_general | solution.py:232
  247.9 15.9 %fusion.21 = bf16[512,1536]{1,0:T(8,128)(2,1)} fusion(f32[10,192]{1,0:T(8,128)S(1)} %select_reduce_fusion, bf16[10,192,1536]{2,1,0:T(8,128)(2,1)} %fusion.26, s32[10,512]{1,0:T(8,128)S(1)} %copy.91, pred[10,512]{1,0:T(8,128)(4,1)S(1)} %get-tuple-element.17), kind=kOutput, calls=%fused_computation.15 | convolution fusion | flops 18128044032 | bytes 7504384 | tf_op jit(solution)/shard_map/esr,esd->rd/dot_general | solution.py:237
  263.9 0.7 compare_reduce_fusion
  264.8 2.9 gather_fusion
  267.9 0.9 copy.93
  268.8 23.4 %reduce-scatter.5.cloned.1.call-done = bf16[128,1536]{1,0:T(8,128)(2,1)} async-done(((bf16[512,1536]{1,0:T(8,128)(2,1)}), bf16[128,1536]{1,0:T(8,128)(2,1)}) %reduce-scatter.5.cloned.1.call-update) | async-done | bytes 393232 | tf_op jit(solution)/shard_map/reduce_scatter | solution.py:244
  (67 shorter events, 4.1 us)
Async XLA Ops:
  7.2 139.6 %copy-start = (bf16[384,1536]{1,0:T(8,128)(2,1)S(1)}, bf16[384,1536]{1,0:T(8,128)(2,1)}, u32[]{:S(2)}) copy-start(bf16[384,1536]{1,0:T(8,128)(2,1)} %param.23) | copy-start | bytes 3538948
  7.2 36.4 %all-gather.5.cloned.1.call-start = ((), (), s32[]{:S(2)}) async-start(), calls=%async_computation.2 | async-start | bytes 1966080 | tf_op jit(solution)/shard_map/all_gather | solution.py:153
  10.4 117.7 %all-gather.7.cloned.1.call-start = ((), (), s32[]{:S(2)}) async-start(), calls=%async_computation.3 | async-start | bytes 4718592 | tf_op jit(solution)/shard_map/all_gather | solution.py:180
  47.0 1.1 copy-start.3
  50.2 143.8 %reduce-scatter.3.cloned.1.call-start = ((), (), s32[]{:S(2)}) async-start(), calls=%async_computation.4 | async-start | bytes 1966080 | tf_op jit(solution)/shard_map/reduce_scatter | solution.py:196
  145.3 48.7 %copy-start.2 = (bf16[128,1536]{1,0:T(8,128)(2,1)S(1)}, bf16[128,1536]{1,0:T(8,128)(2,1)}, u32[]{:S(2)}) copy-start(bf16[128,1536]{1,0:T(8,128)(2,1)} %param.14) | copy-start | bytes 1179652
  145.3 50.0 %copy-start.5 = (f32[1536]{0:T(1024)S(1)}, f32[1536]{0:T(1024)}, u32[]{:S(2)}) copy-start(f32[1536]{0:T(1024)} %param.19) | copy-start | bytes 18436
  145.3 52.0 %copy-start.6 = (f32[128,8]{0,1:T(8,128)S(1)}, f32[128,8]{0,1:T(8,128)}, u32[]{:S(2)}) copy-start(f32[128,8]{0,1:T(8,128)} %param.17) | copy-start | bytes 12292
  145.3 52.0 %copy-start.7 = (s32[128,8]{0,1:T(8,128)S(1)}, s32[128,8]{0,1:T(8,128)}, u32[]{:S(2)}) copy-start(s32[128,8]{0,1:T(8,128)} %param.16) | copy-start | bytes 12292
  148.9 68.1 %all-gather.9.cloned.1.call-start = ((), (), s32[]{:S(2)}) async-start(), calls=%async_computation.5 | async-start | bytes 1966080 | tf_op jit(solution)/shard_map/all_gather | solution.py:213
  197.2 95.0 %reduce-scatter.5.cloned.1.call-start = ((), (), s32[]{:S(2)}) async-start(), calls=%async_computation.6 | async-start | bytes 1966080 | tf_op jit(solution)/shard_map/reduce_scatter | solution.py:244
  247.9 16.0 %copy-start.8 = (s32[64]{0:T(128)S(1)}, s32[64]{0:T(128)}, u32[]{:S(2)}) copy-start(s32[64]{0:T(128)} %param.27) | copy-start | bytes 772
  247.9 19.8 %copy-start.4 = (bf16[12,2,2,64,64]{4,3,2,1,0:T(8,128)(2,1)S(1)}, bf16[12,2,2,64,64]{4,3,2,1,0:T(8,128)(2,1)}, u32[]{:S(2)}) copy-start(bf16[12,2,2,64,64]{4,3,2,1,0:T(8,128)(2,1)} %param.26) | copy-start | bytes 1179652
  247.9 44.3 %copy-start.1 = (bf16[384,1536]{1,0:T(8,128)(2,1)S(1)}, bf16[384,1536]{1,0:T(8,128)(2,1)}, u32[]{:S(2)}) copy-start(bf16[384,1536]{1,0:T(8,128)(2,1)} %param.23) | copy-start | bytes 3538948
Sparse Core Ops, SparseCore 0:
  10.5 20.8 all-gather.4
  50.3 77.7 all-gather.6
  149.0 44.9 reduce-scatter.2
  197.3 19.6 all-gather.8
  264.0 28.1 reduce-scatter.4

commit v2 on v1

--- a/solution.py
+++ b/solution.py
@@ -47,6 +47,23 @@
         ],
         axis=-1,
     )
+
+
+def gather_rows(x, axis_name, axis=0):
+    count = lax.axis_size(axis_name)
+    spread = jnp.broadcast_to(x[None], (count,) + x.shape)
+    got = lax.all_to_all(spread, axis_name, 0, 0, tiled=True)
+    got = jnp.moveaxis(got, 0, axis)
+    shape = list(x.shape)
+    shape[axis] = shape[axis] * count
+    return got.reshape(shape)
+
+
+def scatter_sum_rows(x, axis_name):
+    count = lax.axis_size(axis_name)
+    parts = x.reshape((count, x.shape[0] // count) + x.shape[1:])
+    got = lax.all_to_all(parts, axis_name, 0, 0, tiled=True)
+    return jnp.sum(got.astype(jnp.float32), axis=0)
 
 
 Q_TILE = 128
@@ -142,7 +159,7 @@
     ep_count = lax.axis_size("ep")
     group_len = tok_dev * ep_count
     req_pos = lax.axis_index("req")
-    all_segs = lax.all_gather(seg_ids, ("req", "ep"), axis=0, tiled=True)
+    all_segs = gather_rows(seg_ids, ("req", "ep"))
     all_pos = positions_of(all_segs)
     group_start = req_pos * group_len
     group_pos = lax.dynamic_slice_in_dim(all_pos, group_start, group_len)
@@ -150,7 +167,7 @@
     normed = rms_scale(tokens.astype(jnp.float32), norm1_gain).astype(jnp.bfloat16)
     joined = jnp.concatenate([w_query, key_weight, value_weight], axis=1)
     projected = jnp.dot(
-        lax.all_gather(normed, "ep", axis=0, tiled=True), joined, preferred_element_type=jnp.float32
+        gather_rows(normed, "ep"), joined, preferred_element_type=jnp.float32
     )
     query_width = w_query.shape[1]
     kv_width = key_weight.shape[1]
@@ -177,7 +194,7 @@
     kv_local = jnp.concatenate(
         [key_rows.transpose(1, 0, 2), value_rows.transpose(1, 0, 2)], axis=0
     )
-    kv_all = lax.all_gather(kv_local, "req", axis=1, tiled=True)
+    kv_all = gather_rows(kv_local, "req", axis=1)
     n_rows = kv_all.shape[1]
     q_index = group_start + jnp.arange(group_len, dtype=jnp.int32)
     q_begin = q_index - group_pos
@@ -193,12 +210,10 @@
     picked = jnp.take(kv_paged, block_of, axis=2, mode="clip").transpose(2, 1, 0, 3, 4)
     new_cache = jnp.where(hit[:, None, None, None, None], picked, paged_key_value_cache)
     head_out = head_out.transpose(2, 0, 1, 3).reshape(group_len, query_width)
-    attention = lax.psum_scatter(
+    attention = scatter_sum_rows(
         jnp.dot(head_out, w_out_attn, preferred_element_type=jnp.float32).astype(jnp.bfloat16),
         "ep",
-        scatter_dimension=0,
-        tiled=True,
-    ).astype(jnp.float32)
+    )
     attn_out = attention.astype(jnp.bfloat16)
     moe_in = rms_scale(tokens.astype(jnp.float32) + residual_scale * attention, norm2_gain).astype(
         jnp.bfloat16
@@ -210,8 +225,8 @@
         jnp.where(routes[:, :, None] == expert_ids[None, None, :], route_weights[:, :, None], 0.0),
         axis=1,
     )
-    rows_all = lax.all_gather(moe_in, "ep", axis=0, tiled=True)
-    shares_all = lax.all_gather(shares, "ep", axis=0, tiled=True)
+    rows_all = gather_rows(moe_in, "ep")
+    shares_all = gather_rows(shares, "ep")
     first_expert = lax.axis_index("ep") * exp_here
     shares_here = lax.dynamic_slice_in_dim(shares_all, first_expert, exp_here, 1)
     total_rows = rows_all.shape[0]
@@ -241,9 +256,7 @@
         precision=lax.Precision.HIGHEST,
         preferred_element_type=jnp.float32,
     )
-    moe_out = lax.psum_scatter(
-        partial_rows.astype(jnp.bfloat16), "ep", scatter_dimension=0, tiled=True
-    )
+    moe_out = scatter_sum_rows(partial_rows.astype(jnp.bfloat16), "ep").astype(jnp.bfloat16)
     return (attn_out, moe_out, new_cache)
 
 

time: 300 us -> 265 us (0.88)
  the two profiles are of different devices: /device:TPU:12 before, /device:TPU:16 now
where the time goes in v2:
time: 265 us; the launch traced here: 267 us
  waiting for transfers between devices  107 us (40%)
  matrix products  51 us (19%)
  Pallas kernels  38 us (14%)
  starting transfers between devices  29.6 us (11%)
  local copies, waits for them, and re-layouts  24.9 us (9%)
  other arithmetic  15.5 us (6%)
    all_to_all x5, waiting for transfers between devices, gather_rows(): got = lax.all_to_all(spread, axis_name, 0, 0, tiled=True)  72.9 us
    pallas_call x1, Pallas kernels, flash_attention(): pl.pallas_call(flash_body, grid_spec=grid_spec, out_shape=jax.ShapeDtypeS...  38 us
    all_to_all x2, waiting for transfers between devices, scatter_sum_rows(): got = lax.all_to_all(parts, axis_name, 0, 0, tiled=True)  34 us
    all_to_all x5, starting transfers between devices, gather_rows(): got = lax.all_to_all(spread, axis_name, 0, 0, tiled=True)  22.4 us
    dot_general x1, matrix products, body(): jnp.einsum('esd,edf->esf', arrived, w_in, preferred_element_type=jnp.floa...  16.9 us
    dot_general x1, matrix products, body(): jnp.einsum('esr,esd->rd', dispatch.astype(jnp.float32), weighted, precisi...  15.6 us
    dot_general x1, matrix products, body(): jnp.einsum('esf,efd->esd', activated, w_out, preferred_element_type=jnp.f...  13.6 us
    all_to_all x2, starting transfers between devices, scatter_sum_rows(): got = lax.all_to_all(parts, axis_name, 0, 0, tiled=True)  7.25 us
  transfers between devices with their start and end apart: 7, of which 7 were waited for; matrix products, arithmetic and copies ran while one was open for 10% of the time, Pallas kernels for 0%

profile of v2, /device:TPU:16, one launch (start us, length us, event | category | flops | bytes accessed | tf_op | source)
XLA Modules:
  0.0 266.9 jit_solution(2082241961177532843)
XLA Ops:
  0.7 1.4 broadcast_in_dim.44
  2.0 5.9 %all-to-all-start = ((s32[32,1,128]{2,1,0:T(1,128)}), s32[32,1,128]{2,1,0:T(1,128)S(1)}, u32[]{:S(2)}, u32[]{:S(2)}) async-start(s32[32,1,128]{2,1,0:T(1,128)} %broadcast_in_dim.44), calls=%async_computation | async-start | bytes 32768 | tf_op jit(solution)/shard_map/all_to_all | solution.py:55
  10.3 2.7 all-to-all-done
  14.3 3.6 %all-to-all-start.1 = ((bf16[4,128,1536]{2,1,0:T(8,128)(2,1)}), bf16[4,128,1536]{2,1,0:T(8,128)(2,1)S(1)}, u32[]{:S(2)}, u32[]{:S(2)}) async-start(bf16[4,128,1536]{2,1,0:T(8,128)(2,1)} %broadcast_in_dim.50), calls=%async_computation.1 | async-start | bytes 3145728 | tf_op jit(solution)/shard_map/all_to_all | solution.py:55
  18.9 18.9 %all-to-all-done.1 = bf16[4,128,1536]{2,1,0:T(8,128)(2,1)S(1)} async-done(((bf16[4,128,1536]{2,1,0:T(8,128)(2,1)}), bf16[4,128,1536]{2,1,0:T(8,128)(2,1)S(1)}, u32[]{:S(2)}, u32[]{:S(2)}) %all-to-all-start.1) | async-done | bytes 1572896 | tf_op jit(solution)/shard_map/all_to_all | solution.py:55
  37.9 2.8 %fusion.28 = f32[512,640]{1,0:T(8,128)S(1)} fusion(bf16[512,1536]{1,0:T(8,128)(2,1)S(1)} %bitcast.73, bf16[1536,128]{1,0:T(8,128)(2,1)S(1)} %copy-done.9, bf16[1536,128]{1,0:T(8,128)(2,1)} %param.21, bf16[1536,384]{1,0:T(8,128)(2,1)} %param.20), kind=kOutput, calls=%fused_computation.19 | convolution fusion | flops 1012531200 | bytes 4849664 | tf_op jit(solution)/shard_map/dot_general | solution.py:169
  42.1 1.6 broadcast_in_dim.51
  43.7 5.9 %all-to-all-start.2 = ((bf16[8,4,512,64]{2,3,1,0:T(8,128)(2,1)}), bf16[8,4,512,64]{2,3,1,0:T(8,128)(2,1)S(1)}, u32[]{:S(2)}, u32[]{:S(2)}) async-start(bf16[8,4,512,64]{2,3,1,0:T(8,128)(2,1)} %broadcast_in_dim.51), calls=%async_computation.2 | async-start | bytes 4194304 | tf_op jit(solution)/shard_map/all_to_all | solution.py:55
  52.0 2.1 slice.55
  54.1 2.3 copy.72
  56.4 1.9 subtract_convert_fusion
  58.3 2.1 copy.73
  61.6 2.7 %maximum_bitcast_fusion.q_ref = bf16[2,3,512,64]{3,2,1,0:T(8,128)(2,1)} fusion(bf16[512,2,3,32]{3,0,2,1:T(8,128)(2,1)} %bitcast.70, bf16[512,2,3,32]{3,0,2,1:T(8,128)(2,1)} %bitcast.69), kind=kLoop, calls=%fused_computation.36 | loop fusion | flops 786432 | bytes 786432 | tf_op jit(solution)/shard_map/transpose | solution.py:191
  64.3 30.3 %all-to-all-done.2 = bf16[8,4,512,64]{2,3,1,0:T(8,128)(2,1)S(1)} async-done(((bf16[8,4,512,64]{2,3,1,0:T(8,128)(2,1)}), bf16[8,4,512,64]{2,3,1,0:T(8,128)(2,1)S(1)}, u32[]{:S(2)}, u32[]{:S(2)}) %all-to-all-start.2) | async-done | bytes 2097184 | tf_op jit(solution)/shard_map/all_to_all | solution.py:55
  94.6 3.1 %copy.77 = bf16[4,8,512,64]{3,2,1,0:T(8,128)(2,1)} copy(bf16[4,8,512,64]{2,3,0,1:T(8,128)(2,1)S(1)} %bitcast.66) | data formatting | bytes 4194304 | tf_op jit(solution)/shard_map/transpose | solution.py:56
  97.7 38.0 %shard_map.157 = bf16[2,3,512,64]{3,2,1,0:T(8,128)(2,1)} custom-call(s32[4]{0:T(128)} %get-tuple-element.30.lo_ref, s32[4]{0:T(128)} %get-tuple-element.29.hi_ref, bf16[2,3,512,64]{3,2,1,0:T(8,128)(2,1)} %maximum_bitcast_fusion.q_ref, bf16[4,4096,64]{2,1,0:T(8,128)(2,1)} %bitcast.63, bf16[4,4096,64]{2,1,0:T(8,128)(2,1)} %bitcast.64, ...), custom_call_target="tpu_custom_call" | custom-call | tf_op jit(solution)/shard_map/pallas_call | solution.py:134
  135.7 1.4 copy.79
  137.2 2.2 convolution_convert_fusion
  139.4 3.7 %all-to-all-start.3 = ((bf16[4,128,1536]{2,1,0:T(8,128)(2,1)}), bf16[4,128,1536]{2,1,0:T(8,128)(2,1)S(1)}, u32[]{:S(2)}, u32[]{:S(2)}) async-start(bf16[4,128,1536]{2,1,0:T(8,128)(2,1)} %bitcast.67), calls=%async_computation.3 | async-start | bytes 3145728 | tf_op jit(solution)/shard_map/all_to_all | solution.py:65
  143.1 20.0 %all-to-all-done.3 = bf16[4,128,1536]{2,1,0:T(8,128)(2,1)S(1)} async-done(((bf16[4,128,1536]{2,1,0:T(8,128)(2,1)}), bf16[4,128,1536]{2,1,0:T(8,128)(2,1)S(1)}, u32[]{:S(2)}, u32[]{:S(2)}) %all-to-all-start.3) | async-done | bytes 1572896 | tf_op jit(solution)/shard_map/all_to_all | solution.py:65
  163.7 3.3 %all-to-all-start.4 = ((f32[4,128,40]{1,2,0:T(8,128)}), f32[4,128,40]{1,2,0:T(8,128)S(1)}, u32[]{:S(2)}, u32[]{:S(2)}) async-start(f32[4,128,40]{1,2,0:T(8,128)} %broadcast_in_dim.55), calls=%async_computation.4 | async-start | bytes 163840 | tf_op jit(solution)/shard_map/all_to_all | solution.py:55
  168.4 2.8 %all-to-all-done.4 = f32[4,128,40]{1,2,0:T(8,128)S(1)} async-done(((f32[4,128,40]{1,2,0:T(8,128)}), f32[4,128,40]{1,2,0:T(8,128)S(1)}, u32[]{:S(2)}, u32[]{:S(2)}) %all-to-all-start.4) | async-done | bytes 81952 | tf_op jit(solution)/shard_map/all_to_all | solution.py:55
  171.2 1.3 broadcast_in_dim.56
  172.5 3.7 %all-to-all-start.5 = ((bf16[4,128,1536]{2,1,0:T(8,128)(2,1)}), bf16[4,128,1536]{2,1,0:T(8,128)(2,1)S(1)}, u32[]{:S(2)}, u32[]{:S(2)}) async-start(bf16[4,128,1536]{2,1,0:T(8,128)(2,1)} %broadcast_in_dim.56), calls=%async_computation.5 | async-start | bytes 3145728 | tf_op jit(solution)/shard_map/all_to_all | solution.py:55
  177.9 18.2 %all-to-all-done.5 = bf16[4,128,1536]{2,1,0:T(8,128)(2,1)S(1)} async-done(((bf16[4,128,1536]{2,1,0:T(8,128)(2,1)}), bf16[4,128,1536]{2,1,0:T(8,128)(2,1)S(1)}, u32[]{:S(2)}, u32[]{:S(2)}) %all-to-all-start.5) | async-done | bytes 1572896 | tf_op jit(solution)/shard_map/all_to_all | solution.py:55
  196.1 16.9 %fusion.5 = f32[10,192,1024]{2,1,0:T(8,128)} fusion(bf16[10,1536,1024]{2,1,0:T(8,128)(2,1)} %param.24, bf16[512,1536,1]{1,0,2:T(8,128)(2,1)S(1)} %bitcast.72, s32[10,512]{1,0:T(8,128)S(1)} %copy.82, pred[10,512]{1,0:T(8,128)(4,1)S(1)} %get-tuple-element.17), kind=kOutput, calls=%fused_computation.6 | convolution fusion | flops 9064611840 | bytes 40920064 | tf_op jit(solution)/shard_map/esd,edf->esf/dot_general | solution.py:243
  213.0 13.6 %fusion.26 = bf16[10,192,1536]{2,1,0:T(8,128)(2,1)} fusion(bf16[10,512,1536]{2,1,0:T(8,128)(2,1)} %param.25, f32[10,192,1024]{2,1,0:T(8,128)} %fusion.5), kind=kOutput, calls=%fused_computation.18 | convolution fusion | flops 3025797120 | bytes 29491200 | tf_op jit(solution)/shard_map/esf,efd->esd/dot_general | solution.py:247
  226.6 15.6 %fusion.21 = bf16[512,1536]{1,0:T(8,128)(2,1)} fusion(f32[10,192]{1,0:T(8,128)S(1)} %select_reduce_fusion, bf16[10,192,1536]{2,1,0:T(8,128)(2,1)} %fusion.26, s32[10,512]{1,0:T(8,128)S(1)} %copy.82, pred[10,512]{1,0:T(8,128)(4,1)S(1)} %get-tuple-element.17), kind=kOutput, calls=%fused_computation.16 | convolution fusion | flops 18128044032 | bytes 7504384 | tf_op jit(solution)/shard_map/esr,esd->rd/dot_general | solution.py:252
  242.2 3.6 %all-to-all-start.6 = ((bf16[4,128,1536]{2,1,0:T(8,128)(2,1)}), bf16[4,128,1536]{2,1,0:T(8,128)(2,1)S(1)}, u32[]{:S(2)}, u32[]{:S(2)}) async-start(bf16[4,128,1536]{2,1,0:T(8,128)(2,1)} %bitcast.74), calls=%async_computation.6 | async-start | bytes 3145728 | tf_op jit(solution)/shard_map/all_to_all | solution.py:65
  246.7 2.9 %gather_fusion = bf16[12,2,2,64,64]{4,3,2,1,0:T(8,128)(2,1)S(1)} fusion(bf16[2,2,64,64,64]{4,3,2,1,0:T(8,128)(2,1)} %bitcast.65, s32[1024]{0:T(1024)S(1)} %pad_clamp_fusion), kind=kCustom, calls=%fused_computation | custom fusion | bytes 786480 | tf_op jit(solution)/shard_map/jit(_take)/gather | solution.py:210
  249.5 1.3 bitcast_select_fusion
  251.8 14.0 %all-to-all-done.6 = bf16[4,128,1536]{2,1,0:T(8,128)(2,1)S(1)} async-done(((bf16[4,128,1536]{2,1,0:T(8,128)(2,1)}), bf16[4,128,1536]{2,1,0:T(8,128)(2,1)S(1)}, u32[]{:S(2)}, u32[]{:S(2)}) %all-to-all-start.6) | async-done | bytes 1572896 | tf_op jit(solution)/shard_map/all_to_all | solution.py:65
  (69 shorter events, 16.4 us)
Async XLA Ops:
  0.6 136.5 %copy-start = (bf16[384,1536]{1,0:T(8,128)(2,1)S(1)}, bf16[384,1536]{1,0:T(8,128)(2,1)}, u32[]{:S(2)}) copy-start(bf16[384,1536]{1,0:T(8,128)(2,1)} %param.23) | copy-start | bytes 3538948
  0.6 37.2 %copy-start.9 = (bf16[1536,128]{1,0:T(8,128)(2,1)S(1)}, bf16[1536,128]{1,0:T(8,128)(2,1)}, u32[]{:S(2)}) copy-start(bf16[1536,128]{1,0:T(8,128)(2,1)} %param.22) | copy-start | bytes 1179652
  2.0 10.9 %all-to-all-start = ((s32[32,1,128]{2,1,0:T(1,128)}), s32[32,1,128]{2,1,0:T(1,128)S(1)}, u32[]{:S(2)}, u32[]{:S(2)}) async-start(s32[32,1,128]{2,1,0:T(1,128)} %broadcast_in_dim.44), calls=%async_computation | async-start | bytes 32768 | tf_op jit(solution)/shard_map/all_to_all | solution.py:55
  14.3 23.6 %all-to-all-start.1 = ((bf16[4,128,1536]{2,1,0:T(8,128)(2,1)}), bf16[4,128,1536]{2,1,0:T(8,128)(2,1)S(1)}, u32[]{:S(2)}, u32[]{:S(2)}) async-start(bf16[4,128,1536]{2,1,0:T(8,128)(2,1)} %broadcast_in_dim.50), calls=%async_computation.1 | async-start | bytes 3145728 | tf_op jit(solution)/shard_map/all_to_all | solution.py:55
  18.9 23.1 %copy-start.4 = (f32[512,32]{0,1:T(8,128)}, f32[512,32]{0,1:T(8,128)S(1)}, u32[]{:S(2)}) copy-start(f32[512,32]{0,1:T(8,128)S(1)} %get-tuple-element.28) | copy-start | bytes 196612
  40.7 1.1 copy-start.3
  43.7 50.9 %all-to-all-start.2 = ((bf16[8,4,512,64]{2,3,1,0:T(8,128)(2,1)}), bf16[8,4,512,64]{2,3,1,0:T(8,128)(2,1)S(1)}, u32[]{:S(2)}, u32[]{:S(2)}) async-start(bf16[8,4,512,64]{2,3,1,0:T(8,128)(2,1)} %broadcast_in_dim.51), calls=%async_computation.2 | async-start | bytes 4194304 | tf_op jit(solution)/shard_map/all_to_all | solution.py:55
  135.7 7.3 %copy-start.6 = (f32[128,8]{0,1:T(8,128)S(1)}, f32[128,8]{0,1:T(8,128)}, u32[]{:S(2)}) copy-start(f32[128,8]{0,1:T(8,128)} %param.17) | copy-start | bytes 12292
  135.7 7.3 %copy-start.7 = (s32[128,8]{0,1:T(8,128)S(1)}, s32[128,8]{0,1:T(8,128)}, u32[]{:S(2)}) copy-start(s32[128,8]{0,1:T(8,128)} %param.16) | copy-start | bytes 12292
  137.2 30.1 %copy-start.2 = (bf16[128,1536]{1,0:T(8,128)(2,1)S(1)}, bf16[128,1536]{1,0:T(8,128)(2,1)}, u32[]{:S(2)}) copy-start(bf16[128,1536]{1,0:T(8,128)(2,1)} %param.14) | copy-start | bytes 1179652
  139.3 28.2 %copy-start.5 = (f32[1536]{0:T(1024)S(1)}, f32[1536]{0:T(1024)}, u32[]{:S(2)}) copy-start(f32[1536]{0:T(1024)} %param.19) | copy-start | bytes 18436
  139.4 23.7 %all-to-all-start.3 = ((bf16[4,128,1536]{2,1,0:T(8,128)(2,1)}), bf16[4,128,1536]{2,1,0:T(8,128)(2,1)S(1)}, u32[]{:S(2)}, u32[]{:S(2)}) async-start(bf16[4,128,1536]{2,1,0:T(8,128)(2,1)} %bitcast.67), calls=%async_computation.3 | async-start | bytes 3145728 | tf_op jit(solution)/shard_map/all_to_all | solution.py:65
  163.7 7.5 %all-to-all-start.4 = ((f32[4,128,40]{1,2,0:T(8,128)}), f32[4,128,40]{1,2,0:T(8,128)S(1)}, u32[]{:S(2)}, u32[]{:S(2)}) async-start(f32[4,128,40]{1,2,0:T(8,128)} %broadcast_in_dim.55), calls=%async_computation.4 | async-start | bytes 163840 | tf_op jit(solution)/shard_map/all_to_all | solution.py:55
  172.5 23.6 %all-to-all-start.5 = ((bf16[4,128,1536]{2,1,0:T(8,128)(2,1)}), bf16[4,128,1536]{2,1,0:T(8,128)(2,1)S(1)}, u32[]{:S(2)}, u32[]{:S(2)}) async-start(bf16[4,128,1536]{2,1,0:T(8,128)(2,1)} %broadcast_in_dim.56), calls=%async_computation.5 | async-start | bytes 3145728 | tf_op jit(solution)/shard_map/all_to_all | solution.py:55
  226.6 19.2 %copy-start.8 = (s32[64]{0:T(128)S(1)}, s32[64]{0:T(128)}, u32[]{:S(2)}) copy-start(s32[64]{0:T(128)} %param.27) | copy-start | bytes 772
  242.2 23.6 %all-to-all-start.6 = ((bf16[4,128,1536]{2,1,0:T(8,128)(2,1)}), bf16[4,128,1536]{2,1,0:T(8,128)(2,1)S(1)}, u32[]{:S(2)}, u32[]{:S(2)}) async-start(bf16[4,128,1536]{2,1,0:T(8,128)(2,1)} %bitcast.74), calls=%async_computation.6 | async-start | bytes 3145728 | tf_op jit(solution)/shard_map/all_to_all | solution.py:65
  245.7 21.1 %copy-start.1 = (bf16[384,1536]{1,0:T(8,128)(2,1)S(1)}, bf16[384,1536]{1,0:T(8,128)(2,1)}, u32[]{:S(2)}) copy-start(bf16[384,1536]{1,0:T(8,128)(2,1)} %param.23) | copy-start | bytes 3538948
